TPU v7x, 512 devices: a whole 4x4x16 slice. The times are simulated.
512 devices in a mesh: rep: 32 (over z_lo, x), seq: 16 (over z_hi, y, core).
Axes of the slice: x: 4, y: 4, z: 16 (z_hi: 2, z_lo: 8; z = z_hi * 8 + z_lo), core: 2. Of those that a mesh axis runs over, the one named last changes fastest.
Arguments:
- tokens: bfloat16 [32, 4096, 6144], P('rep', 'seq'), may hold values from -6 to 6
- queries: bfloat16 [32, 4096, 128], P('rep', 'seq'), may hold values from -4 to 4
- ctx_grad: bfloat16 [32, 4096, 128], P('rep', 'seq'), may hold values from -0.25 to 0.25
- kv_weight: bfloat16 [32, 6144, 256], P('rep', 'seq'), may hold values from -0.078125 to 0.078125
- rand_blocks: int32 [64, 3], replicated, may hold values from 0 to 63
- step_count: int32 [1], replicated, may hold values from 0 to 63
Outputs:
- mixed_update: float32 [32, 6144, 256], P('rep', 'seq')
- query_grad: bfloat16 [32, 4096, 128], P('rep', 'seq')
Inputs may be any that keep to these rules, and one draw needn't show every extreme that they name: `rand_blocks`: block indices of the same replica sequence.
All inputs are finite; a program needn't handle non-finite values.
Results may differ from a plain program's by a relative error of at most 0.02.
Values may be sent and summed in bfloat16 or wider, within the bound.
No kernel may reach another device: no remote copies, remote signals or barrier semaphores. Data moves between devices by JAX's collectives and lax.ppermute only.
A program may use at most 64 MiB of HBM per device.

v0:
```python
from functools import partial
import jax
import jax.numpy as jnp
from jax import lax
from jax.sharding import PartitionSpec as P

BLOCK = 64


def for_sending(value):

    def short(part):
        return part.astype(jnp.bfloat16) if part.dtype == jnp.float32 else part

    return jax.tree.map(short, value)


def shifted(value, axis, steps):
    count = lax.axis_size(axis)
    pairs = [(source, (source + steps) % count) for source in range(count)]
    return lax.ppermute(value, axis, pairs)


def fold_rows(tok_rows, row_piece):
    return jnp.dot(tok_rows, row_piece, preferred_element_type=jnp.float32)


def contract_rows(matrix_a, matrix_b):
    return lax.dot_general(
        matrix_a, matrix_b, (((0,), (0,)), ((), ())), preferred_element_type=jnp.float32
    )


def contract_cols(matrix_a, matrix_b):
    return lax.dot_general(
        matrix_a, matrix_b, (((1,), (1,)), ((), ())), preferred_element_type=jnp.float32
    )


def attend_mask(query_blocks, key_blocks, chosen_rows, blk_size):
    is_near = jnp.abs(query_blocks[:, None] - key_blocks[None, :]) <= 1
    picked = jnp.any(chosen_rows[:, :, None] == key_blocks[None, None, :], axis=1)
    allowed = is_near | (key_blocks[None, :] == 0) | picked
    return jnp.repeat(jnp.repeat(allowed, blk_size, axis=0), blk_size, axis=1)


def gossip(update, distance, rep_count):
    if distance == 0:
        return update
    from_low = jax.tree.map(
        lambda part, own: part.astype(own.dtype),
        shifted(for_sending(update), "rep", distance),
        update,
    )
    from_high = jax.tree.map(
        lambda part, own: part.astype(own.dtype),
        shifted(for_sending(update), "rep", rep_count - distance),
        update,
    )
    return (update + from_low + from_high) / 3.0


def per_device(tokens, queries, ctx_grad, kv_weight, rand_blocks, step_count):
    tokens_here = tokens[0]
    query_here = queries[0]
    grad_here = ctx_grad[0]
    weight_here = kv_weight[0]
    seq_count = lax.axis_size("seq")
    rep_count = lax.axis_size("rep")
    seq_index = lax.axis_index("seq")
    tok_count = tokens_here.shape[0]
    kv_width = weight_here.shape[1]
    head_size = kv_width // 2
    blk_size = BLOCK
    blocks_dev = tok_count // blk_size
    block_count = blocks_dev * seq_count
    inv_root = head_size ** (-0.5)
    kv_here = fold_rows(tokens_here, lax.all_gather(weight_here, "seq", axis=0, tiled=True)).astype(
        jnp.bfloat16
    )
    kv_all = lax.all_gather(kv_here, "seq", axis=0, tiled=True)
    keys_all = kv_all[:, :head_size]
    values_all = kv_all[:, head_size:]
    blocks_here = seq_index * blocks_dev + jnp.arange(blocks_dev, dtype=jnp.int32)
    every_block = jnp.arange(block_count, dtype=jnp.int32)
    chosen_here = lax.dynamic_slice_in_dim(rand_blocks, seq_index * blocks_dev, blocks_dev, 0)
    allowed = attend_mask(blocks_here, every_block, chosen_here, blk_size)
    scores = contract_cols(query_here, keys_all) * inv_root
    unnorm = jnp.where(allowed, jnp.exp(scores), jnp.float32(0.0))
    row_total = jnp.sum(unnorm, axis=1, keepdims=True)
    prob_rows = unnorm / row_total
    prob_low = prob_rows.astype(jnp.bfloat16)
    context = jnp.dot(prob_low, values_all, preferred_element_type=jnp.float32)
    row_delta = jnp.sum(grad_here.astype(jnp.float32) * context, axis=1, keepdims=True)
    prob_grad = contract_cols(grad_here, values_all)
    score_grad = (prob_rows * (prob_grad - row_delta) * inv_root).astype(jnp.bfloat16)
    query_grad = jnp.dot(score_grad, keys_all, preferred_element_type=jnp.float32).astype(
        jnp.bfloat16
    )
    key_terms = contract_rows(score_grad, query_here)
    value_terms = contract_rows(prob_low, grad_here)
    grad_terms = jnp.concatenate([key_terms, value_terms], axis=1).reshape(
        seq_count, tok_count, kv_width
    )
    received = lax.all_to_all(
        grad_terms.astype(jnp.bfloat16), "seq", split_axis=0, concat_axis=0, tiled=True
    ).astype(grad_terms.dtype)
    kv_grad = jnp.sum(received, axis=0).astype(jnp.bfloat16)
    grad_slice = lax.psum_scatter(
        contract_rows(tokens_here, kv_grad).astype(jnp.bfloat16),
        "seq",
        scatter_dimension=0,
        tiled=True,
    ).astype(jnp.float32)
    branches = [
        partial(gossip, distance=(1 << level_idx) % rep_count, rep_count=rep_count)
        for level_idx in range(4)
    ]
    mixed_update = lax.switch(step_count[0] % 4, branches, grad_slice)
    return (mixed_update[None], query_grad[None])


def solution(mesh):
    return jax.shard_map(
        per_device,
        mesh=mesh,
        in_specs=(
            P("rep", "seq", None),
            P("rep", "seq", None),
            P("rep", "seq", None),
            P("rep", "seq", None),
            P(),
            P(),
        ),
        out_specs=(P("rep", "seq", None), P("rep", "seq", None)),
        check_vma=False,
    )
```

profile of v0, /device:TPU:8, one launch (start us, length us, event | category | flops | bytes accessed | tf_op | source)
XLA Modules:
  0.0 498.9 jit_solution(13018875669005355405)
XLA Ops:
  7.2 0.0 copy-start
  7.2 0.0 all-gather.6.cloned.1.call-start
  7.2 0.7 all-gather.6.cloned.1.call-update
  7.9 0.0 all-gather.4.cloned.1.call-start
  8.0 114.0 %all-gather.6.cloned.1.call-done = bf16[1,6144,256]{2,1,0:T(8,128)(2,1)} async-done(((bf16[1,384,256]{2,1,0:T(8,128)(2,1)}), bf16[1,6144,256]{2,1,0:T(8,128)(2,1)}) %all-gather.6.cloned.1.call-update) | async-done | bytes 3145744 | tf_op jit(solution)/shard_map/all_gather | solution.py:78
  121.9 3.5 fusion.13
  125.5 0.0 all-gather.4.cloned.1.call-update
  125.5 0.0 reduce-scatter.4.cloned.1.call-start
  125.6 0.0 copy-done.6
  125.6 0.1 constant_dynamic-slice_fusion
  125.7 0.1 fusion.28
  125.7 0.1 fusion.30
  125.8 0.1 copy.22
  125.9 0.1 broadcast_in_dim.33
  126.1 0.1 reshape.24
  126.2 0.0 copy-done.5
  126.2 0.1 copy.23
  126.3 82.9 %all-gather.4.cloned.1.call-done = bf16[4096,256]{1,0:T(8,128)(2,1)} async-done(((bf16[256,256]{1,0:T(8,128)(2,1)}), bf16[4096,256]{1,0:T(8,128)(2,1)}) %all-gather.4.cloned.1.call-update) | async-done | bytes 2097168 | tf_op jit(solution)/shard_map/all_gather | solution.py:81
  209.2 0.3 broadcast_in_dim.34
  209.5 2.4 fusion.31
  211.9 0.3 fusion.12
  212.2 0.8 convolution_convert_fusion.1
  213.0 0.8 copy-done.2
  213.8 0.6 fusion.18
  214.4 0.8 fusion.7
  215.2 0.8 convolution_convert_fusion.2
  216.0 0.2 pad_maximum_fusion
  216.2 0.3 copy-done.1
  216.5 0.2 copy.35
  216.7 50.3 %all_to_all.5 = bf16[16,256,256]{1,2,0:T(8,128)(2,1)} all-to-all(bf16[16,256,256]{1,2,0:T(8,128)(2,1)S(1)} %bitcast.69), channel_id=1, replica_groups=mesh['rep'=32,'seq'=16] {'seq'}, dimensions={0} | all-to-all | bytes 4194304 | tf_op jit(solution)/shard_map/all_to_all | solution.py:105
  267.0 1.9 reduce_sum.32
  268.9 2.7 fusion
  271.5 4.6 copy.30
  276.2 0.0 reduce-scatter.4.cloned.1.call-update
  276.9 3.2 fusion.19
  280.1 184.1 %reduce-scatter.4.cloned.1.call-done = bf16[384,256]{1,0:T(8,128)(2,1)} async-done(((bf16[6144,256]{1,0:T(8,128)(2,1)}), bf16[384,256]{1,0:T(8,128)(2,1)}) %reduce-scatter.4.cloned.1.call-update) | async-done | bytes 196624
  464.2 1.7 copy.31
  466.0 1.0 convert_element_type.89
  466.9 24.7 %conditional.1 = (f32[1,384,256]{2,1,0:T(8,128)S(1)}) conditional(s32[]{:T(128)} %clamp.3, f32[384,256]{0,1:T(8,128)S(1)} %convert_element_type.89, f32[384,256]{0,1:T(8,128)S(1)} %convert_element_type.89, f32[384,256]{0,1:T(8,128)S(1)} %convert_element_type.89, f32[384,256]{0,1:T(8,128)S(1)} %convert_element_type.89), branch_computations={%region_5.6_spmd, %region_6.7_spmd, %region_7.8_spmd, %region_8.9_... | conditional | flops 589824 | bytes 4128856 | solution.py:119
  467.0 0.9 copy.27
  467.9 1.0 convert_element_type.64
  468.9 5.1 %collective-permute-start.3 = (bf16[384,256]{1,0:T(8,128)(2,1)S(1)}, bf16[384,256]{1,0:T(8,128)(2,1)S(1)}, u32[]{:S(2)}, u32[]{:S(2)}) collective-permute-start(bf16[384,256]{1,0:T(8,128)(2,1)S(1)} %convert_element_type.64), channel_id=1, source_target_pairs={{0,480},{16,496},{32,0},{48,16},{64,32},{80,48},{96,64},{112,80},{... | collective-permute-start | bytes 589832 | tf_op jit(solution)/shard_map/cond/branch_1_fun/ppermute | solution.py:21
  474.0 2.3 collective-permute-start.2
  476.3 1.7 collective-permute-done.3
  478.0 12.6 %collective-permute-done.2 = bf16[384,256]{1,0:T(8,128)(2,1)S(1)} collective-permute-done((bf16[384,256]{1,0:T(8,128)(2,1)S(1)}, bf16[384,256]{1,0:T(8,128)(2,1)S(1)}, u32[]{:S(2)}, u32[]{:S(2)}) %collective-permute-start.2) | collective-permute-done | bytes 196640 | tf_op jit(solution)/shard_map/cond/branch_1_fun/ppermute | solution.py:21
  490.6 1.1 multiply_bitcast_fusion.1
  491.7 0.0 copy-start.3
  491.7 0.7 copy-done.3
  (9 shorter events, 0.0 us)
Async XLA Ops:
  7.2 114.8 %copy-start = (bf16[1,256,6144]{2,1,0:T(8,128)(2,1)S(1)}, bf16[1,256,6144]{2,1,0:T(8,128)(2,1)}, u32[]{:S(2)}) copy-start(bf16[1,256,6144]{2,1,0:T(8,128)(2,1)} %param.10) | copy-start | bytes 9437188
  7.2 114.8 %all-gather.6.cloned.1.call-start = ((), (), s32[]{:S(2)}) async-start(), calls=%async_computation.3 | async-start | bytes 3342336 | tf_op jit(solution)/shard_map/all_gather | solution.py:78
  7.9 117.7 %copy-start.6 = (s32[64,3]{0,1:T(4,128)S(1)}, s32[64,3]{0,1:T(4,128)}, u32[]{:S(2)}) copy-start(s32[64,3]{0,1:T(4,128)} %param.14) | copy-start | bytes 2308
  7.9 118.3 %copy-start.5 = (bf16[1,256,128]{2,1,0:T(8,128)(2,1)S(1)}, bf16[1,256,128]{2,1,0:T(8,128)(2,1)}, u32[]{:S(2)}) copy-start(bf16[1,256,128]{2,1,0:T(8,128)(2,1)} %param.12) | copy-start | bytes 196612
  7.9 201.5 %copy-start.4 = (bf16[1,256,128]{2,1,0:T(8,128)(2,1)S(1)}, bf16[1,256,128]{2,1,0:T(8,128)(2,1)}, u32[]{:S(2)}) copy-start(bf16[1,256,128]{2,1,0:T(8,128)(2,1)} %param.11) | copy-start | bytes 196612
  7.9 201.2 %all-gather.4.cloned.1.call-start = ((), (), s32[]{:S(2)}) async-start(), calls=%async_computation.2 | async-start | bytes 2228224 | tf_op jit(solution)/shard_map/all_gather | solution.py:81
  125.5 338.7 %reduce-scatter.4.cloned.1.call-start = ((), (), s32[]{:S(2)}) async-start(), calls=%async_computation.4 | async-start | bytes 3342336
  212.2 1.6 copy-start.2
  215.2 1.4 copy-start.1
  468.9 9.1 %collective-permute-start.3 = (bf16[384,256]{1,0:T(8,128)(2,1)S(1)}, bf16[384,256]{1,0:T(8,128)(2,1)S(1)}, u32[]{:S(2)}, u32[]{:S(2)}) collective-permute-start(bf16[384,256]{1,0:T(8,128)(2,1)S(1)} %convert_element_type.64), channel_id=1, source_target_pairs={{0,480},{16,496},{32,0},{48,16},{64,32},{80,48},{96,64},{112,80},{... | collective-permute-start | bytes 589832 | tf_op jit(solution)/shard_map/cond/branch_1_fun/ppermute | solution.py:21
  474.0 16.6 %collective-permute-start.2 = (bf16[384,256]{1,0:T(8,128)(2,1)S(1)}, bf16[384,256]{1,0:T(8,128)(2,1)S(1)}, u32[]{:S(2)}, u32[]{:S(2)}) collective-permute-start(bf16[384,256]{1,0:T(8,128)(2,1)S(1)} %convert_element_type.64), channel_id=1, source_target_pairs={{0,32},{16,48},{32,64},{48,80},{64,96},{80,112},{96,128},{112,144}... | collective-permute-start | bytes 589832 | tf_op jit(solution)/shard_map/cond/branch_1_fun/ppermute | solution.py:21
  491.7 0.7 copy-start.3
Sparse Core Ops, SparseCore 0:
  11.3 110.5 all-gather.5
  125.8 83.3 all-gather.3
  276.3 187.8 reduce-scatter.3
where the time goes:
time: 499 us
  waiting for transfers between devices  396 us (79%)
  blocking collectives  50.3 us (10%)
  matrix products  14.8 us (3%)
  between operations  14.6 us (3%)
  local copies, waits for them, and re-layouts  10.2 us (2%)
  starting transfers between devices  7.46 us (1%)
  other arithmetic  5.65 us (1%)
    unnamed x4, waiting for transfers between devices  185 us
    all_gather x1, waiting for transfers between devices, per_device(): lax.all_gather(weight_here, 'seq', axis=0, tiled=True)  114 us
    all_gather x1, waiting for transfers between devices, per_device(): kv_all = lax.all_gather(kv_here, 'seq', axis=0, tiled=True)  82.9 us
    all_to_all x1, blocking collectives, per_device(): lax.all_to_all(grad_terms.astype(jnp.bfloat16), 'seq', split_axis=0, conc...  50.3 us
    ppermute x2, waiting for transfers between devices, shifted(): return lax.ppermute(value, axis, pairs)  14.3 us
  transfers between devices with their start and end apart: 5, of which 5 were waited for; matrix products, arithmetic and copies ran while one was open for 1% of the time, Pallas kernels for 0%

commit v1 on v0

--- a/solution.py
+++ b/solution.py
@@ -75,9 +75,12 @@
     blocks_dev = tok_count // blk_size
     block_count = blocks_dev * seq_count
     inv_root = head_size ** (-0.5)
-    kv_here = fold_rows(tokens_here, lax.all_gather(weight_here, "seq", axis=0, tiled=True)).astype(
-        jnp.bfloat16
-    )
+    kv_here = fold_rows(
+        tokens_here,
+        jnp.concatenate(
+            lax.all_to_all(jnp.stack([weight_here] * lax.axis_size("seq")), "seq", 0, 0), axis=0
+        ),
+    ).astype(jnp.bfloat16)
     kv_all = lax.all_gather(kv_here, "seq", axis=0, tiled=True)
     keys_all = kv_all[:, :head_size]
     values_all = kv_all[:, head_size:]

time: 499 us -> 551 us (1.10)
  blocking collectives: 50.3 us -> 138 us
  waiting for transfers between devices: 396 us -> 360 us
    all_gather x1 -> x0, waiting for transfers between devices: 114 us -> none  [per_device(): lax.all_gather(weight_here, 'seq', axis=0, tiled=True)]
    all_to_all x0 -> x1, blocking collectives: none -> 87.7 us  [per_device(): lax.all_to_all(jnp.stack([weight_here] * lax.axis_size('seq')), 'seq', 0, 0)]
    all_gather x1, waiting for transfers between devices: 82.9 us -> 161 us  [per_device(): kv_all = lax.all_gather(kv_here, 'seq', axis=0, tiled=True)]
    unnamed x4 -> x3, waiting for transfers between devices: 185 us -> 184 us
  transfers between devices with their start and end apart: 5 -> 4, of which waited for: 5 -> 4; matrix products, arithmetic and copies ran while one was open for 1% -> 1% of each run, Pallas kernels for 0% -> 0%
where the time goes in v1:
time: 551 us; the launch traced here: 550 us
  waiting for transfers between devices  360 us (65%)
  blocking collectives  138 us (25%)
  between operations  14.9 us (3%)
  matrix products  12.9 us (2%)
  local copies, waits for them, and re-layouts  11.5 us (2%)
  starting transfers between devices  7.43 us (1%)
  other arithmetic  5.65 us (1%)
    unnamed x3, waiting for transfers between devices  184 us
    all_gather x1, waiting for transfers between devices, per_device(): kv_all = lax.all_gather(kv_here, 'seq', axis=0, tiled=True)  161 us
    all_to_all x1, blocking collectives, per_device(): lax.all_to_all(jnp.stack([weight_here] * lax.axis_size('seq')), 'seq', 0, 0)  87.7 us
    all_to_all x1, blocking collectives, per_device(): lax.all_to_all(grad_terms.astype(jnp.bfloat16), 'seq', split_axis=0, conc...  50.4 us
    ppermute x2, waiting for transfers between devices, shifted(): return lax.ppermute(value, axis, pairs)  14.3 us
  transfers between devices with their start and end apart: 4, of which 4 were waited for; matrix products, arithmetic and copies ran while one was open for 1% of the time, Pallas kernels for 0%

profile of v1, /device:TPU:8, one launch (start us, length us, event | category | flops | bytes accessed | tf_op | source)
XLA Modules:
  0.0 550.4 jit_solution(17984893096840618144)
XLA Ops:
  7.2 0.0 copy-start
  7.2 0.0 all-gather.2.cloned.1.call-start
  7.2 1.4 stack.3
  8.6 87.7 %all_to_all.10 = bf16[16,384,256]{2,1,0:T(8,128)(2,1)S(1)} all-to-all(bf16[16,384,256]{2,1,0:T(8,128)(2,1)S(1)} %stack.3), channel_id=1, replica_groups=mesh['rep'=32,'seq'=16] {'seq'}, dimensions={0} | all-to-all | bytes 6291456 | tf_op jit(solution)/shard_map/all_to_all | solution.py:81
  96.3 1.7 fusion.12
  98.0 0.0 all-gather.2.cloned.1.call-update
  98.0 0.0 reduce-scatter.4.cloned.1.call-start
  98.1 0.0 copy-done.6
  98.1 0.1 constant_dynamic-slice_fusion
  98.2 0.1 fusion.25
  98.3 0.1 fusion.27
  98.4 0.1 copy.22
  98.5 0.1 broadcast_in_dim.33
  98.6 0.1 reshape.28
  98.7 0.0 copy-done.5
  98.7 0.1 copy.23
  98.9 161.5 %all-gather.2.cloned.1.call-done = bf16[4096,256]{1,0:T(8,128)(2,1)} async-done(((bf16[256,256]{1,0:T(8,128)(2,1)}), bf16[4096,256]{1,0:T(8,128)(2,1)}) %all-gather.2.cloned.1.call-update) | async-done | bytes 2097168 | tf_op jit(solution)/shard_map/all_gather | solution.py:84
  260.3 0.3 broadcast_in_dim.34
  260.6 2.4 fusion.28
  263.0 0.3 fusion.11
  263.3 0.0 copy-start.2
  263.4 0.8 convolution_convert_fusion.1
  264.2 0.8 copy-done.2
  264.9 0.6 fusion.15
  265.5 0.8 fusion.7
  266.3 0.8 convolution_convert_fusion.2
  267.1 0.2 pad_maximum_fusion
  267.3 0.3 copy-done.1
  267.7 0.2 copy.35
  267.9 50.4 %all_to_all.11 = bf16[16,256,256]{1,2,0:T(8,128)(2,1)} all-to-all(bf16[16,256,256]{1,2,0:T(8,128)(2,1)S(1)} %bitcast.67), channel_id=1, replica_groups=mesh['rep'=32,'seq'=16] {'seq'}, dimensions={0} | all-to-all | bytes 4194304 | tf_op jit(solution)/shard_map/all_to_all | solution.py:108
  318.3 1.9 reduce_sum.32
  320.2 2.7 fusion
  322.9 4.6 copy.30
  327.5 0.0 reduce-scatter.4.cloned.1.call-update
  328.2 3.2 fusion.16
  331.4 184.0 %reduce-scatter.4.cloned.1.call-done = bf16[384,256]{1,0:T(8,128)(2,1)} async-done(((bf16[6144,256]{1,0:T(8,128)(2,1)}), bf16[384,256]{1,0:T(8,128)(2,1)}) %reduce-scatter.4.cloned.1.call-update) | async-done | bytes 196624
  515.4 1.7 copy.31
  517.1 1.0 convert_element_type.89
  518.1 24.7 %conditional.1 = (f32[1,384,256]{2,1,0:T(8,128)S(1)}) conditional(s32[]{:T(128)} %clamp.3, f32[384,256]{0,1:T(8,128)S(1)} %convert_element_type.89, f32[384,256]{0,1:T(8,128)S(1)} %convert_element_type.89, f32[384,256]{0,1:T(8,128)S(1)} %convert_element_type.89, f32[384,256]{0,1:T(8,128)S(1)} %convert_element_type.89), branch_computations={%region_5.6_spmd, %region_6.7_spmd, %region_7.8_spmd, %region_8.9_... | conditional | flops 589824 | bytes 4128856 | solution.py:122
  518.1 0.9 copy.27
  519.0 1.0 convert_element_type.64
  520.1 5.0 collective-permute-start.3
  525.1 2.3 collective-permute-start.2
  527.4 1.7 collective-permute-done.3
  529.1 12.6 %collective-permute-done.2 = bf16[384,256]{1,0:T(8,128)(2,1)S(1)} collective-permute-done((bf16[384,256]{1,0:T(8,128)(2,1)S(1)}, bf16[384,256]{1,0:T(8,128)(2,1)S(1)}, u32[]{:S(2)}, u32[]{:S(2)}) %collective-permute-start.2) | collective-permute-done | bytes 196640 | tf_op jit(solution)/shard_map/cond/branch_1_fun/ppermute | solution.py:21
  541.7 1.1 multiply_bitcast_fusion.1
  542.8 0.0 copy-start.3
  542.8 0.7 copy-done.3
  (8 shorter events, 0.0 us)
Async XLA Ops:
  7.2 89.2 %copy-start = (bf16[1,256,6144]{2,1,0:T(8,128)(2,1)S(1)}, bf16[1,256,6144]{2,1,0:T(8,128)(2,1)}, u32[]{:S(2)}) copy-start(bf16[1,256,6144]{2,1,0:T(8,128)(2,1)} %param.10) | copy-start | bytes 9437188
  7.2 253.1 %all-gather.2.cloned.1.call-start = ((), (), s32[]{:S(2)}) async-start(), calls=%async_computation.3 | async-start | bytes 2228224 | tf_op jit(solution)/shard_map/all_gather | solution.py:84
  96.3 1.8 copy-start.6
  96.3 2.4 copy-start.5
  96.3 164.3 %copy-start.4 = (bf16[1,256,128]{2,1,0:T(8,128)(2,1)S(1)}, bf16[1,256,128]{2,1,0:T(8,128)(2,1)}, u32[]{:S(2)}) copy-start(bf16[1,256,128]{2,1,0:T(8,128)(2,1)} %param.11) | copy-start | bytes 196612
  98.0 417.4 %reduce-scatter.4.cloned.1.call-start = ((), (), s32[]{:S(2)}) async-start(), calls=%async_computation.4 | async-start | bytes 3342336
  263.3 1.6 copy-start.2
  266.3 1.4 copy-start.1
  520.1 9.1 %collective-permute-start.3 = (bf16[384,256]{1,0:T(8,128)(2,1)S(1)}, bf16[384,256]{1,0:T(8,128)(2,1)S(1)}, u32[]{:S(2)}, u32[]{:S(2)}) collective-permute-start(bf16[384,256]{1,0:T(8,128)(2,1)S(1)} %convert_element_type.64), channel_id=1, source_target_pairs={{0,480},{16,496},{32,0},{48,16},{64,32},{80,48},{96,64},{112,80},{... | collective-permute-start | bytes 589832 | tf_op jit(solution)/shard_map/cond/branch_1_fun/ppermute | solution.py:21
  525.1 16.6 %collective-permute-start.2 = (bf16[384,256]{1,0:T(8,128)(2,1)S(1)}, bf16[384,256]{1,0:T(8,128)(2,1)S(1)}, u32[]{:S(2)}, u32[]{:S(2)}) collective-permute-start(bf16[384,256]{1,0:T(8,128)(2,1)S(1)} %convert_element_type.64), channel_id=1, source_target_pairs={{0,32},{16,48},{32,64},{48,80},{64,96},{80,112},{96,128},{112,144}... | collective-permute-start | bytes 589832 | tf_op jit(solution)/shard_map/cond/branch_1_fun/ppermute | solution.py:21
  542.8 0.7 copy-start.3
Sparse Core Ops, SparseCore 0:
  98.1 162.1 all-gather.1
  327.6 187.7 reduce-scatter.3
